TPU v7x, 32 devices: a whole 2x2x4 slice. The times are simulated.
32 devices in a mesh: visit: 8 (over z, x), sky: 4 (over y, core).
Axes of the slice: x: 2, y: 2, z: 4, core: 2. Of those that a mesh axis runs over, the one named last changes fastest.
Arguments:
- warped: bfloat16 [16, 512, 2048], P('visit', 'sky'), may hold values from -11 to 21
- inv_var: bfloat16 [16, 512, 2048], P('visit', 'sky'), may hold values from 0.19921875 to 5
- intersection: int32 [8, 4, 4], P('visit', 'sky'), may hold values from 0 to 3, as said below
- col_start: int32 [8, 4], P('visit', 'sky'), may hold values from 0 to 1536, as said below
- row_interp: bfloat16 [8, 4, 512, 512], P('visit', 'sky'), may hold values from -0.22 to 1.4, as said below
- col_interp: bfloat16 [8, 4, 512, 512], P('visit', 'sky'), may hold values from -0.22 to 1.4, as said below
- cell_ids: int32 [8, 4, 4, 4], P('visit', 'sky'), may hold values from 0 to 15
- kernels: bfloat16 [8, 4, 16, 121], P('visit', 'sky'), may hold values from -0.59765625 to 0.59765625
- science: bfloat16 [8, 4, 512, 512], P('visit', 'sky'), may hold values from -8 to 8
- inv_sigma: bfloat16 [8, 4, 512, 512], P('visit', 'sky'), may hold values from 0.29882812 to 1
Outputs:
- coadd: float32 [512, 2048], P('sky')
- outlier_weight: float32 [8, 4, 512, 512], P('visit', 'sky')
Inputs may be any that keep to these rules, and one draw needn't show every extreme that they name: `intersection`: the 4 strip numbers of one tile are distinct. `col_start`: a multiple of 128. `row_interp`: nonzero only within two places of the diagonal, each row's diagonal entry larger than the sum of its other magnitudes. `col_interp`: nonzero only within two places of the diagonal, each row's diagonal entry larger than the sum of its other magnitudes.
All inputs are finite; a program needn't handle non-finite values.
Results may differ from a plain program's by a relative error of at most 0.0017.
Values may be sent and summed in bfloat16 or wider, within the bound.
No kernel may reach another device: no remote copies, remote signals or barrier semaphores. Data moves between devices by JAX's collectives and lax.ppermute only.
A program may use at most 64 MiB of HBM per device.

v0:
```python
import jax
import jax.numpy as jnp
from jax import lax
from jax.sharding import PartitionSpec as P

STRIP = 128
NOV = 4
TILE = 512
KSIZE = 11
CELL = 128
NCELL = 16
PASSES = 3
CAUCHY = 2.0
OUTLIER = 3.0


def local_coadd(values, weights):
    root_weight = jnp.sqrt(weights)
    coadd_field = jnp.sum(weights * values, axis=0) / jnp.sum(weights, axis=0)
    for pass_index in range(PASSES):
        scaled = (values - coadd_field[None]) * root_weight / CAUCHY
        cauchy = weights / (1.0 + scaled * scaled)
        coadd_field = jnp.sum(cauchy * values, axis=0) / jnp.sum(cauchy, axis=0)
    return coadd_field


def psf_match(blotted, cell_grid, kernel_table):
    tile_side = blotted.shape[1]
    blocks = tile_side // CELL
    half_width = KSIZE // 2
    window = CELL + KSIZE - 1
    picker = (cell_grid.reshape(-1)[:, None] == jnp.arange(NCELL, dtype=jnp.int32)[None, :]).astype(
        jnp.bfloat16
    )
    tap_rows = jnp.dot(picker, kernel_table, preferred_element_type=jnp.float32)
    tap_rows = tap_rows.astype(jnp.bfloat16).reshape(blocks * blocks, KSIZE, KSIZE)
    source = jnp.arange(window, dtype=jnp.int32)[:, None]
    target = jnp.arange(CELL, dtype=jnp.int32)[None, :]
    diagonal = (
        (source - target)[None] == jnp.arange(KSIZE, dtype=jnp.int32)[:, None, None]
    ).astype(jnp.bfloat16)
    banded_all = jnp.einsum(
        "kab,bcl->kcal", tap_rows, diagonal, preferred_element_type=jnp.float32
    ).astype(jnp.bfloat16)
    banded_all = banded_all.reshape(blocks * blocks, window, KSIZE * CELL)
    padded = jnp.pad(blotted, ((half_width, half_width), (half_width, half_width)))
    row_parts = []
    for row_block in range(blocks):
        rows_window = lax.slice_in_dim(padded, row_block * CELL, row_block * CELL + window, axis=0)
        col_parts = []
        for col_block in range(blocks):
            cols_window = lax.slice_in_dim(
                rows_window, col_block * CELL, col_block * CELL + window, axis=1
            )
            horizontal = jnp.dot(
                cols_window,
                banded_all[row_block * blocks + col_block],
                preferred_element_type=jnp.float32,
            ).reshape(window, KSIZE, CELL)
            summed = horizontal[0:CELL, 0, :]
            for tap_row in range(1, KSIZE):
                summed = summed + horizontal[tap_row : tap_row + CELL, tap_row, :]
            col_parts.append(summed)
        row_parts.append(jnp.concatenate(col_parts, axis=1))
    return jnp.concatenate(row_parts, axis=0)


def shards(
    warped,
    inv_var,
    intersection,
    col_start,
    row_interp,
    col_interp,
    cell_ids,
    kernels,
    science,
    inv_sigma,
):
    n_visit = lax.axis_size("visit")
    n_sky = lax.axis_size("sky")
    local_visits, strip_rows, sky_w = warped.shape
    stacked = jnp.stack([warped, inv_var], axis=0)
    chunk = strip_rows // n_visit
    stacked = stacked.reshape(2, local_visits, n_visit, chunk, sky_w).transpose(2, 0, 1, 3, 4)
    stacked = stacked.reshape(n_visit, 2 * local_visits * chunk, sky_w)
    gathered = lax.all_to_all(stacked, "visit", split_axis=0, concat_axis=0, tiled=True)
    gathered = gathered.reshape(n_visit, 2, local_visits, chunk, sky_w)
    gathered = gathered.transpose(1, 0, 2, 3, 4).reshape(2, n_visit * local_visits, chunk, sky_w)
    row_share = local_coadd(gathered[0].astype(jnp.float32), gathered[1].astype(jnp.float32))
    copies = jnp.broadcast_to(row_share[None], (n_visit,) + row_share.shape)
    coadd_field = lax.all_to_all(copies, "visit", split_axis=0, concat_axis=0, tiled=True)
    coadd_field = coadd_field.reshape(n_visit * chunk, sky_w)
    coadd_low = coadd_field.astype(jnp.bfloat16)
    start_col = col_start[0, 0]
    all_starts = lax.all_gather(col_start[0], "sky", axis=0, tiled=True)
    windows = jnp.stack(
        [lax.dynamic_slice_in_dim(coadd_low, all_starts[peer], TILE, 1) for peer in range(n_sky)],
        axis=0,
    )
    strips_here = lax.all_to_all(windows, "sky", split_axis=0, concat_axis=0, tiled=True)
    strips = intersection[0, 0]
    footprint = jnp.concatenate(
        [
            lax.dynamic_index_in_dim(strips_here, strips[slot], 0, keepdims=False)
            for slot in range(NOV)
        ],
        axis=0,
    )
    projected = jnp.dot(row_interp[0, 0], footprint, preferred_element_type=jnp.float32).astype(
        jnp.bfloat16
    )
    blotted = jnp.dot(projected, col_interp[0, 0], preferred_element_type=jnp.float32).astype(
        jnp.bfloat16
    )
    matched = psf_match(blotted, cell_ids[0, 0], kernels[0, 0])
    residual = (
        (science[0, 0].astype(jnp.float32) - matched)
        * inv_sigma[0, 0].astype(jnp.float32)
        / OUTLIER
    )
    outlier = 1.0 / (1.0 + residual * residual)
    return (coadd_field, outlier[None, None])


def solution(mesh):
    in_specs = (
        P("visit", "sky", None),
        P("visit", "sky", None),
        P("visit", "sky", None),
        P("visit", "sky"),
        P("visit", "sky", None, None),
        P("visit", "sky", None, None),
        P("visit", "sky", None, None),
        P("visit", "sky", None, None),
        P("visit", "sky", None, None),
        P("visit", "sky", None, None),
    )
    out_specs = (P("sky", None), P("visit", "sky", None, None))
    return jax.shard_map(shards, mesh=mesh, in_specs=in_specs, out_specs=out_specs, check_vma=False)
```

profile of v0, /device:TPU:0, one launch (start us, length us, event | category | flops | bytes accessed | tf_op | source)
XLA Modules:
  0.0 227.3 jit_solution(4613131695956559904)
XLA Ops:
  0.6 1.8 maximum_bitcast_fusion
  2.7 55.3 %all_to_all.15 = bf16[8,64,2048]{2,1,0:T(8,128)(2,1)S(1)} all-to-all(bf16[8,64,2048]{2,1,0:T(8,128)(2,1)S(1)} %bitcast.262), channel_id=1, replica_groups=mesh['visit'=8,'sky'=4] {'visit'}, dimensions={0} | all-to-all | bytes 4194304 | tf_op jit(solution)/shard_map/all_to_all | solution.py:87
  58.4 1.3 fusion.23
  59.8 1.3 fusion.24
  61.1 1.3 fusion.25
  62.5 1.1 broadcast_in_dim.2
  63.6 3.6 %all-to-all-start.1 = ((f32[8,16,2048]{2,1,0:T(8,128)}), f32[8,16,2048]{2,1,0:T(8,128)S(1)}, u32[]{:S(2)}, u32[]{:S(2)}) async-start(f32[8,16,2048]{2,1,0:T(8,128)} %broadcast_in_dim.2), calls=%async_computation.1 | async-start | bytes 2097152 | tf_op jit(solution)/shard_map/all_to_all | solution.py:92
  69.1 5.0 %all-reduce.1 = s32[4]{0:T(128)S(1)} all-reduce(s32[4]{0:T(128)S(1)} %bitcast_dynamic-update-slice_fusion), channel_id=2, replica_groups=mesh['visit'=8,'sky'=4] {'sky'}, use_global_device_ids=true, to_apply=%add.1 | all-reduce | flops 4 | bytes 32
  82.8 4.4 %convert_bitcast_fusion = bf16[16,138,11,128]{3,0,2,1:T(8,128)(2,1)} fusion(s32[138,128]{1,0:T(8,128)S(1)} %iota_subtract_fusion, bf16[16,11,11]{2,1,0:T(8,128)(2,1)S(1)} %reshape.203), kind=kOutput, calls=%fused_computation | convolution fusion | flops 71698176 | bytes 6292256 | tf_op jit(solution)/shard_map/kab,bcl->kcal/dot_general | solution.py:42
  87.2 5.6 %all-to-all-done.1 = f32[8,16,2048]{2,1,0:T(8,128)S(1)} async-done(((f32[8,16,2048]{2,1,0:T(8,128)}), f32[8,16,2048]{2,1,0:T(8,128)S(1)}, u32[]{:S(2)}, u32[]{:S(2)}) %all-to-all-start.1) | async-done | bytes 1048608 | tf_op jit(solution)/shard_map/all_to_all | solution.py:92
  93.1 0.9 pad_maximum_fusion
  94.0 4.3 %all-to-all-start.2 = ((bf16[4,128,512]{2,1,0:T(8,128)(2,1)}), bf16[4,128,512]{2,1,0:T(8,128)(2,1)}, u32[]{:S(2)}, u32[]{:S(2)}) async-start(bf16[4,128,512]{2,1,0:T(8,128)(2,1)} %pad_maximum_fusion), calls=%async_computation.2 | async-start | bytes 1048576 | tf_op jit(solution)/shard_map/all_to_all | solution.py:101
  98.4 46.7 %slice_reduce_fusion.15 = (bf16[138,11,128]{2,1,0:T(8,128)(2,1)}, bf16[138,11,128]{2,1,0:T(8,128)(2,1)}, bf16[138,11,128]{2,1,0:T(8,128)(2,1)}, bf16[138,11,128]...) fusion(bf16[16,138,11,128]{3,0,2,1:T(8,128)(2,1)} %convert_bitc, ...), kind=kLoop, calls=%fused_computation.56 | loop fusion | bytes 12435456 | tf_op jit(solution)/shard_map/slice | solution.py:57
  150.4 1.2 pad.35
  152.5 2.1 dot_general.129
  154.5 1.2 pad.50
  156.6 2.1 dot_general.174
  158.6 1.2 pad.49
  160.7 2.1 dot_general.171
  162.8 1.2 pad.48
  164.8 2.1 dot_general.168
  166.9 1.2 pad.47
  168.9 2.1 dot_general.165
  171.0 1.2 pad.46
  173.0 2.1 dot_general.162
  175.1 1.2 pad.45
  177.1 2.1 dot_general.159
  179.2 1.2 pad.44
  180.3 0.9 copy.58
  181.2 2.1 dot_general.156
  183.3 1.2 pad.43
  185.3 2.1 dot_general.153
  187.4 1.2 pad.42
  189.4 2.1 dot_general.150
  191.5 1.2 pad.41
  193.6 2.1 dot_general.147
  195.6 1.2 pad.40
  197.7 2.1 dot_general.144
  199.8 1.2 pad.39
  200.9 0.9 copy.53
  201.8 2.1 dot_general.141
  204.9 1.3 dot_general.138
  206.6 1.1 dot_general.132
  207.7 1.1 dot_general.135
  211.2 1.8 dynamic-slice_bitcast_fusion.3
  213.0 2.1 convolution_convert_fusion
  225.0 1.3 fusion.22
  226.3 1.0 copy.104
  (113 shorter events, 24.4 us)
Async XLA Ops:
  0.6 212.4 %copy-start = (bf16[1,1,512,512]{3,2,1,0:T(8,128)(2,1)S(1)}, bf16[1,1,512,512]{3,2,1,0:T(8,128)(2,1)}, u32[]{:S(2)}) copy-start(bf16[1,1,512,512]{3,2,1,0:T(8,128)(2,1)} %param.15) | copy-start | bytes 1572868
  62.4 5.4 %copy-start.21 = (u32[32]{0:T(128)S(1)}, u32[32]{0:T(128)}, u32[]{:S(2)}) copy-start(u32[32]{0:T(128)} %constant.44) | copy-start | bytes 388
  62.5 17.4 %copy-start.19 = (s32[1,1,4,4]{3,2,1,0:T(4,128)S(1)}, s32[1,1,4,4]{3,2,1,0:T(4,128)}, u32[]{:S(2)}) copy-start(s32[1,1,4,4]{3,2,1,0:T(4,128)} %param.16) | copy-start | bytes 196
  62.5 17.4 %copy-start.20 = (bf16[1,1,16,121]{3,2,1,0:T(8,128)(2,1)S(1)}, bf16[1,1,16,121]{3,2,1,0:T(8,128)(2,1)}, u32[]{:S(2)}) copy-start(bf16[1,1,16,121]{3,2,1,0:T(8,128)(2,1)} %param.17) | copy-start | bytes 11620
  63.6 29.2 %all-to-all-start.1 = ((f32[8,16,2048]{2,1,0:T(8,128)}), f32[8,16,2048]{2,1,0:T(8,128)S(1)}, u32[]{:S(2)}, u32[]{:S(2)}) async-start(f32[8,16,2048]{2,1,0:T(8,128)} %broadcast_in_dim.2), calls=%async_computation.1 | async-start | bytes 2097152 | tf_op jit(solution)/shard_map/all_to_all | solution.py:92
  94.0 117.1 %all-to-all-start.2 = ((bf16[4,128,512]{2,1,0:T(8,128)(2,1)}), bf16[4,128,512]{2,1,0:T(8,128)(2,1)}, u32[]{:S(2)}, u32[]{:S(2)}) async-start(bf16[4,128,512]{2,1,0:T(8,128)(2,1)} %pad_maximum_fusion), calls=%async_computation.2 | async-start | bytes 1048576 | tf_op jit(solution)/shard_map/all_to_all | solution.py:101
  98.4 46.7 %copy-start.18 = (s32[1,1,4]{2,1,0:T(1,128)S(1)}, s32[1,1,4]{2,1,0:T(1,128)}, u32[]{:S(2)}) copy-start(s32[1,1,4]{2,1,0:T(1,128)} %param.12) | copy-start | bytes 52
  213.0 2.1 copy-start.1
  215.1 1.1 copy-start.2
  215.1 1.4 copy-start.3
  216.2 1.1 copy-start.4
  216.6 1.1 copy-start.5
  217.3 1.1 copy-start.6
  217.7 1.1 copy-start.7
  218.4 1.1 copy-start.8
  219.0 1.1 copy-start.9
  219.5 1.1 copy-start.10
  220.1 1.1 copy-start.11
  220.6 1.1 copy-start.12
  221.2 1.1 copy-start.13
  222.3 1.1 copy-start.15
  222.7 1.1 copy-start.14
  223.8 1.0 copy-start.16
  223.8 1.2 copy-start.17
where the time goes:
time: 229 us; the launch traced here: 227 us
  local copies, waits for them, and re-layouts  115 us (50%)
  blocking collectives  60.3 us (26%)
  between operations  16.8 us (7%)
  matrix products  11.7 us (5%)
  other arithmetic  9.64 us (4%)
  starting transfers between devices  7.91 us (3%)
  waiting for transfers between devices  5.6 us (2%)
    all_to_all x1, blocking collectives, shards(): lax.all_to_all(stacked, 'visit', split_axis=0, concat_axis=0, tiled=True)  55.3 us
    slice x1, local copies, waits for them, and re-layouts, psf_match(): banded_all[row_block * blocks + col_block]  46.7 us
    unnamed x80, local copies, waits for them, and re-layouts  33.4 us
    dot_general x16, local copies, waits for them, and re-layouts, psf_match(): jnp.dot(cols_window, banded_all[row_block * blocks + col_block], preferre...  30.4 us
    all_to_all x1, waiting for transfers between devices, shards(): lax.all_to_all(copies, 'visit', split_axis=0, concat_axis=0, tiled=True)  5.6 us
    dot_general x16, matrix products, psf_match(): jnp.dot(cols_window, banded_all[row_block * blocks + col_block], preferre...  5.03 us
    unnamed x1, blocking collectives  4.97 us
  transfers between devices with their start and end apart: 2, of which 1 were waited for; matrix products, arithmetic and copies ran while one was open for 49% of the time, Pallas kernels for 0%

commit v1 on v0

--- a/solution.py
+++ b/solution.py
@@ -12,6 +12,17 @@
 PASSES = 3
 CAUCHY = 2.0
 OUTLIER = 3.0
+
+
+def cut_along(value, dim, size):
+    before, after = (value.shape[:dim], value.shape[dim + 1 :])
+    return jnp.moveaxis(value.reshape(*before, size, -1, *after), dim, 0)
+
+
+def laid_out(parts, dim):
+    parts = jnp.moveaxis(parts, 0, dim)
+    shape = parts.shape
+    return parts.reshape(*shape[:dim], shape[dim] * shape[dim + 1], *shape[dim + 2 :])
 
 
 def local_coadd(values, weights):
@@ -84,7 +95,14 @@
     chunk = strip_rows // n_visit
     stacked = stacked.reshape(2, local_visits, n_visit, chunk, sky_w).transpose(2, 0, 1, 3, 4)
     stacked = stacked.reshape(n_visit, 2 * local_visits * chunk, sky_w)
-    gathered = lax.all_to_all(stacked, "visit", split_axis=0, concat_axis=0, tiled=True)
+    length, mine = (lax.axis_size("visit"), lax.axis_index("visit"))
+    pieces = cut_along(stacked, 0, length)
+    outs = [pieces[mine]]
+    for step in range(1, length):
+        sent = pieces[mine ^ step]
+        outs.append(lax.ppermute(sent, "visit", [(i, i ^ step) for i in range(length)]))
+    pieces = jnp.stack(outs)[mine ^ jnp.arange(length)]
+    gathered = laid_out(pieces, 0)
     gathered = gathered.reshape(n_visit, 2, local_visits, chunk, sky_w)
     gathered = gathered.transpose(1, 0, 2, 3, 4).reshape(2, n_visit * local_visits, chunk, sky_w)
     row_share = local_coadd(gathered[0].astype(jnp.float32), gathered[1].astype(jnp.float32))

time: 229 us -> 236 us (1.031)
  blocking collectives: 60.3 us -> 4.97 us
  waiting for transfers between devices: 5.6 us -> 43.2 us
  starting transfers between devices: 7.91 us -> 21.2 us
  local copies, waits for them, and re-layouts: 115 us -> 126 us
    all_to_all x1 -> x0, blocking collectives: 55.3 us -> none  [shards(): lax.all_to_all(stacked, 'visit', split_axis=0, concat_axis=0, tiled=True)]
    ppermute x0 -> x7, waiting for transfers between devices: none -> 38.7 us  [shards(): lax.ppermute(sent, 'visit', [(i, i ^ step) for i in range(length)])]
    ppermute x0 -> x7, starting transfers between devices: none -> 14 us  [shards(): lax.ppermute(sent, 'visit', [(i, i ^ step) for i in range(length)])]
    unnamed x80 -> x88, local copies, waits for them, and re-layouts: 33.4 us -> 40.2 us
  transfers between devices with their start and end apart: 2 -> 9, of which waited for: 1 -> 4; matrix products, arithmetic and copies ran while one was open for 49% -> 51% of each run, Pallas kernels for 0% -> 0%
where the time goes in v1:
time: 236 us; the launch traced here: 234 us
  local copies, waits for them, and re-layouts  126 us (53%)
  waiting for transfers between devices  43.2 us (18%)
  starting transfers between devices  21.2 us (9%)
  between operations  16.5 us (7%)
  matrix products  11.7 us (5%)
  other arithmetic  9.92 us (4%)
  blocking collectives  4.97 us (2%)
    slice x1, local copies, waits for them, and re-layouts, psf_match(): banded_all[row_block * blocks + col_block]  46.8 us
    unnamed x88, local copies, waits for them, and re-layouts  40.2 us
    ppermute x7, waiting for transfers between devices, shards(): lax.ppermute(sent, 'visit', [(i, i ^ step) for i in range(length)])  38.7 us
    dot_general x16, local copies, waits for them, and re-layouts, psf_match(): jnp.dot(cols_window, banded_all[row_block * blocks + col_block], preferre...  31.4 us
    ppermute x7, starting transfers between devices, shards(): lax.ppermute(sent, 'visit', [(i, i ^ step) for i in range(length)])  14 us
    dot_general x16, matrix products, psf_match(): jnp.dot(cols_window, banded_all[row_block * blocks + col_block], preferre...  5.05 us
    unnamed x1, blocking collectives  4.97 us
  transfers between devices with their start and end apart: 9, of which 4 were waited for; matrix products, arithmetic and copies ran while one was open for 51% of the time, Pallas kernels for 0%

profile of v1, /device:TPU:0, one launch (start us, length us, event | category | flops | bytes accessed | tf_op | source)
XLA Modules:
  0.0 233.7 jit_solution(7272458129251025500)
XLA Ops:
  0.7 1.8 maximum_bitcast_fusion
  3.6 3.0 %collective-permute-start = (bf16[1,64,2048]{2,1,0:T(8,128)(2,1)S(1)}, bf16[1,64,2048]{2,1,0:T(8,128)(2,1)S(1)}, u32[]{:S(2)}, u32[]{:S(2)}) collective-permute-start(bf16[1,64,2048]{2,1,0:T(8,128)(2,1)S(1)} %get-tuple-element.32), channel_id=1, source_target_pairs={{0,4},{4,0},{8,12},{12,8},{16,20},{20,16},{24,28},{28,24},{1,5},{5... | collective-permute-start | bytes 786440 | tf_op jit(solution)/shard_map/ppermute | solution.py:103
  6.6 3.6 %collective-permute-start.6 = (bf16[1,64,2048]{2,1,0:T(8,128)(2,1)S(1)}, bf16[1,64,2048]{2,1,0:T(8,128)(2,1)S(1)}, u32[]{:S(2)}, u32[]{:S(2)}) collective-permute-start(bf16[1,64,2048]{2,1,0:T(8,128)(2,1)S(1)} %get-tuple-element.26), channel_id=1, source_target_pairs={{0,28},{4,24},{8,20},{12,16},{16,12},{20,8},{24,4},{28,0},{1,29},{... | collective-permute-start | bytes 786440 | tf_op jit(solution)/shard_map/ppermute | solution.py:103
  10.2 1.9 collective-permute-start.4
  12.1 2.1 collective-permute-start.3
  14.2 4.2 %collective-permute-done = bf16[1,64,2048]{2,1,0:T(8,128)(2,1)S(1)} collective-permute-done((bf16[1,64,2048]{2,1,0:T(8,128)(2,1)S(1)}, bf16[1,64,2048]{2,1,0:T(8,128)(2,1)S(1)}, u32[]{:S(2)}, u32[]{:S(2)}) %collective-permute-start) | collective-permute-done | bytes 262176 | tf_op jit(solution)/shard_map/ppermute | solution.py:103
  19.2 18.8 %collective-permute-done.1 = bf16[1,64,2048]{2,1,0:T(8,128)(2,1)S(1)} collective-permute-done((bf16[1,64,2048]{2,1,0:T(8,128)(2,1)S(1)}, bf16[1,64,2048]{2,1,0:T(8,128)(2,1)S(1)}, u32[]{:S(2)}, u32[]{:S(2)}) %collective-permute-start.1) | collective-permute-done | bytes 262176 | tf_op jit(solution)/shard_map/ppermute | solution.py:103
  37.9 3.4 %collective-permute-start.2 = (bf16[1,64,2048]{2,1,0:T(8,128)(2,1)S(1)}, bf16[1,64,2048]{2,1,0:T(8,128)(2,1)S(1)}, u32[]{:S(2)}, u32[]{:S(2)}) collective-permute-start(bf16[1,64,2048]{2,1,0:T(8,128)(2,1)S(1)} %get-tuple-element.30), channel_id=1, source_target_pairs={{0,12},{4,8},{8,4},{12,0},{16,28},{20,24},{24,20},{28,16},{1,13},{... | collective-permute-start | bytes 786440 | tf_op jit(solution)/shard_map/ppermute | solution.py:103
  42.1 15.7 %collective-permute-done.2 = bf16[1,64,2048]{2,1,0:T(8,128)(2,1)S(1)} collective-permute-done((bf16[1,64,2048]{2,1,0:T(8,128)(2,1)S(1)}, bf16[1,64,2048]{2,1,0:T(8,128)(2,1)S(1)}, u32[]{:S(2)}, u32[]{:S(2)}) %collective-permute-start.2) | collective-permute-done | bytes 262176 | tf_op jit(solution)/shard_map/ppermute | solution.py:103
  61.5 2.3 gather_fusion
  64.2 1.3 fusion.23
  65.5 1.3 fusion.24
  66.9 1.3 fusion.25
  69.3 3.6 %all-to-all-start = ((f32[8,16,2048]{2,1,0:T(8,128)}), f32[8,16,2048]{2,1,0:T(8,128)S(1)}, u32[]{:S(2)}, u32[]{:S(2)}) async-start(f32[8,16,2048]{2,1,0:T(8,128)} %broadcast_in_dim.2), calls=%async_computation | async-start | bytes 2097152 | tf_op jit(solution)/shard_map/all_to_all | solution.py:110
  74.8 5.0 %all-reduce.1 = s32[4]{0:T(128)S(1)} all-reduce(s32[4]{0:T(128)S(1)} %bitcast_dynamic-update-slice_fusion.7), channel_id=2, replica_groups=mesh['visit'=8,'sky'=4] {'sky'}, use_global_device_ids=true, to_apply=%add.1 | all-reduce | flops 4 | bytes 32
  88.5 4.4 %convert_bitcast_fusion = bf16[16,138,11,128]{3,0,2,1:T(8,128)(2,1)} fusion(s32[138,128]{1,0:T(8,128)S(1)} %iota_subtract_fusion, bf16[16,11,11]{2,1,0:T(8,128)(2,1)S(1)} %reshape.211), kind=kOutput, calls=%fused_computation.1 | convolution fusion | flops 71698176 | bytes 6292256 | tf_op jit(solution)/shard_map/kab,bcl->kcal/dot_general | solution.py:53
  92.9 4.5 %all-to-all-done = f32[8,16,2048]{2,1,0:T(8,128)S(1)} async-done(((f32[8,16,2048]{2,1,0:T(8,128)}), f32[8,16,2048]{2,1,0:T(8,128)S(1)}, u32[]{:S(2)}, u32[]{:S(2)}) %all-to-all-start) | async-done | bytes 1048608 | tf_op jit(solution)/shard_map/all_to_all | solution.py:110
  98.7 3.6 %all-to-all-start.1 = ((bf16[4,128,512]{2,1,0:T(8,128)(2,1)}), bf16[4,128,512]{2,1,0:T(8,128)(2,1)S(1)}, u32[]{:S(2)}, u32[]{:S(2)}) async-start(bf16[4,128,512]{2,1,0:T(8,128)(2,1)} %pad_maximum_fusion), calls=%async_computation.1 | async-start | bytes 1048576 | tf_op jit(solution)/shard_map/all_to_all | solution.py:119
  102.3 46.8 %slice_reduce_fusion.15 = (bf16[138,11,128]{2,1,0:T(8,128)(2,1)}, bf16[138,11,128]{2,1,0:T(8,128)(2,1)}, bf16[138,11,128]{2,1,0:T(8,128)(2,1)}, bf16[138,11,128]...) fusion(bf16[16,138,11,128]{3,0,2,1:T(8,128)(2,1)} %convert_bitc, ...), kind=kLoop, calls=%fused_computation.57 | loop fusion | bytes 12435456 | tf_op jit(solution)/shard_map/slice | solution.py:68
  154.5 1.2 pad.36
  156.5 2.1 dot_general.129
  158.6 1.2 pad.51
  160.6 2.1 dot_general.174
  162.7 1.2 pad.50
  164.7 2.1 dot_general.171
  166.8 1.2 pad.49
  168.8 2.1 dot_general.168
  170.9 1.2 pad.48
  172.9 2.1 dot_general.165
  175.0 1.2 pad.47
  177.0 2.1 dot_general.162
  179.1 1.2 pad.46
  181.1 2.1 dot_general.159
  185.3 2.1 dot_general.156
  189.4 2.1 dot_general.153
  191.4 1.2 pad.43
  193.5 2.1 dot_general.150
  195.6 1.2 pad.42
  197.6 2.1 dot_general.147
  199.7 1.2 pad.41
  201.7 2.1 dot_general.144
  203.8 1.2 pad.40
  205.8 2.1 dot_general.141
  207.9 1.2 pad.39
  210.0 2.1 dot_general.138
  214.0 1.3 dot_general.132
  219.5 2.1 convolution_convert_fusion
  231.5 1.3 fusion.22
  (139 shorter events, 40.9 us)
Async XLA Ops:
  0.6 218.8 %copy-start = (bf16[1,1,512,512]{3,2,1,0:T(8,128)(2,1)S(1)}, bf16[1,1,512,512]{3,2,1,0:T(8,128)(2,1)}, u32[]{:S(2)}) copy-start(bf16[1,1,512,512]{3,2,1,0:T(8,128)(2,1)} %param.15) | copy-start | bytes 1572868
  3.6 14.9 %collective-permute-start = (bf16[1,64,2048]{2,1,0:T(8,128)(2,1)S(1)}, bf16[1,64,2048]{2,1,0:T(8,128)(2,1)S(1)}, u32[]{:S(2)}, u32[]{:S(2)}) collective-permute-start(bf16[1,64,2048]{2,1,0:T(8,128)(2,1)S(1)} %get-tuple-element.32), channel_id=1, source_target_pairs={{0,4},{4,0},{8,12},{12,8},{16,20},{20,16},{24,28},{28,24},{1,5},{5... | collective-permute-start | bytes 786440 | tf_op jit(solution)/shard_map/ppermute | solution.py:103
  6.6 54.2 %collective-permute-start.6 = (bf16[1,64,2048]{2,1,0:T(8,128)(2,1)S(1)}, bf16[1,64,2048]{2,1,0:T(8,128)(2,1)S(1)}, u32[]{:S(2)}, u32[]{:S(2)}) collective-permute-start(bf16[1,64,2048]{2,1,0:T(8,128)(2,1)S(1)} %get-tuple-element.26), channel_id=1, source_target_pairs={{0,28},{4,24},{8,20},{12,16},{16,12},{20,8},{24,4},{28,0},{1,29},{... | collective-permute-start | bytes 786440 | tf_op jit(solution)/shard_map/ppermute | solution.py:103
  10.1 49.9 %collective-permute-start.5 = (bf16[1,64,2048]{2,1,0:T(8,128)(2,1)S(1)}, bf16[1,64,2048]{2,1,0:T(8,128)(2,1)S(1)}, u32[]{:S(2)}, u32[]{:S(2)}) collective-permute-start(bf16[1,64,2048]{2,1,0:T(8,128)(2,1)S(1)} %get-tuple-element.27), channel_id=1, source_target_pairs={{0,24},{4,28},{8,16},{12,20},{16,8},{20,12},{24,0},{28,4},{1,25},{... | collective-permute-start | bytes 786440 | tf_op jit(solution)/shard_map/ppermute | solution.py:103
  10.2 49.1 %collective-permute-start.4 = (bf16[1,64,2048]{2,1,0:T(8,128)(2,1)S(1)}, bf16[1,64,2048]{2,1,0:T(8,128)(2,1)S(1)}, u32[]{:S(2)}, u32[]{:S(2)}) collective-permute-start(bf16[1,64,2048]{2,1,0:T(8,128)(2,1)S(1)} %get-tuple-element.28), channel_id=1, source_target_pairs={{0,20},{4,16},{8,28},{12,24},{16,4},{20,0},{24,12},{28,8},{1,21},{... | collective-permute-start | bytes 786440 | tf_op jit(solution)/shard_map/ppermute | solution.py:103
  12.1 46.4 %collective-permute-start.3 = (bf16[1,64,2048]{2,1,0:T(8,128)(2,1)S(1)}, bf16[1,64,2048]{2,1,0:T(8,128)(2,1)S(1)}, u32[]{:S(2)}, u32[]{:S(2)}) collective-permute-start(bf16[1,64,2048]{2,1,0:T(8,128)(2,1)S(1)} %get-tuple-element.29), channel_id=1, source_target_pairs={{0,16},{4,20},{8,24},{12,28},{16,0},{20,4},{24,8},{28,12},{1,17},{... | collective-permute-start | bytes 786440 | tf_op jit(solution)/shard_map/ppermute | solution.py:103
  18.5 19.5 %collective-permute-start.1 = (bf16[1,64,2048]{2,1,0:T(8,128)(2,1)S(1)}, bf16[1,64,2048]{2,1,0:T(8,128)(2,1)S(1)}, u32[]{:S(2)}, u32[]{:S(2)}) collective-permute-start(bf16[1,64,2048]{2,1,0:T(8,128)(2,1)S(1)} %get-tuple-element.31), channel_id=1, source_target_pairs={{0,8},{4,12},{8,0},{12,4},{16,24},{20,28},{24,16},{28,20},{1,9},{5... | collective-permute-start | bytes 786440 | tf_op jit(solution)/shard_map/ppermute | solution.py:103
  37.9 19.9 %collective-permute-start.2 = (bf16[1,64,2048]{2,1,0:T(8,128)(2,1)S(1)}, bf16[1,64,2048]{2,1,0:T(8,128)(2,1)S(1)}, u32[]{:S(2)}, u32[]{:S(2)}) collective-permute-start(bf16[1,64,2048]{2,1,0:T(8,128)(2,1)S(1)} %get-tuple-element.30), channel_id=1, source_target_pairs={{0,12},{4,8},{8,4},{12,0},{16,28},{20,24},{24,20},{28,16},{1,13},{... | collective-permute-start | bytes 786440 | tf_op jit(solution)/shard_map/ppermute | solution.py:103
  68.2 5.4 %copy-start.22 = (u32[32]{0:T(128)S(1)}, u32[32]{0:T(128)}, u32[]{:S(2)}) copy-start(u32[32]{0:T(128)} %constant.67) | copy-start | bytes 388
  68.2 17.3 %copy-start.20 = (s32[1,1,4,4]{3,2,1,0:T(4,128)S(1)}, s32[1,1,4,4]{3,2,1,0:T(4,128)}, u32[]{:S(2)}) copy-start(s32[1,1,4,4]{3,2,1,0:T(4,128)} %param.16) | copy-start | bytes 196
  68.2 17.4 %copy-start.21 = (bf16[1,1,16,121]{3,2,1,0:T(8,128)(2,1)S(1)}, bf16[1,1,16,121]{3,2,1,0:T(8,128)(2,1)}, u32[]{:S(2)}) copy-start(bf16[1,1,16,121]{3,2,1,0:T(8,128)(2,1)} %param.17) | copy-start | bytes 11620
  69.3 28.1 %all-to-all-start = ((f32[8,16,2048]{2,1,0:T(8,128)}), f32[8,16,2048]{2,1,0:T(8,128)S(1)}, u32[]{:S(2)}, u32[]{:S(2)}) async-start(f32[8,16,2048]{2,1,0:T(8,128)} %broadcast_in_dim.2), calls=%async_computation | async-start | bytes 2097152 | tf_op jit(solution)/shard_map/all_to_all | solution.py:110
  98.7 120.0 %all-to-all-start.1 = ((bf16[4,128,512]{2,1,0:T(8,128)(2,1)}), bf16[4,128,512]{2,1,0:T(8,128)(2,1)S(1)}, u32[]{:S(2)}, u32[]{:S(2)}) async-start(bf16[4,128,512]{2,1,0:T(8,128)(2,1)} %pad_maximum_fusion), calls=%async_computation.1 | async-start | bytes 1048576 | tf_op jit(solution)/shard_map/all_to_all | solution.py:119
  102.3 46.9 %copy-start.19 = (s32[1,1,4]{2,1,0:T(1,128)S(1)}, s32[1,1,4]{2,1,0:T(1,128)}, u32[]{:S(2)}) copy-start(s32[1,1,4]{2,1,0:T(1,128)} %param.12) | copy-start | bytes 52
  213.2 2.1 copy-start.16
  219.5 2.1 copy-start.1
  221.6 1.1 copy-start.2
  221.6 1.4 copy-start.3
  222.6 1.1 copy-start.4
  223.0 1.1 copy-start.5
  223.7 1.1 copy-start.6
  224.1 1.3 copy-start.7
  224.8 1.1 copy-start.8
  225.5 1.1 copy-start.9
  225.9 1.1 copy-start.10
  226.6 1.1 copy-start.11
  227.0 1.1 copy-start.12
  227.7 1.1 copy-start.13
  228.1 1.1 copy-start.14
  228.8 1.1 copy-start.15
  230.3 1.0 copy-start.17
  230.3 1.2 copy-start.18
